TPU v7x, 32 devices: a whole 2x2x4 slice. The times are simulated.
32 devices in a mesh: grp: 2 (over y), ctx: 8 (over z, x), pair: 2 (over core).
Axes of the slice: x: 2, y: 2, z: 4, core: 2. Of those that a mesh axis runs over, the one named last changes fastest.
Arguments:
- normed_input: bfloat16 [4, 1024, 2688], P(('grp', 'pair'), 'ctx'), parts along dimension 0, may hold values from -6 to 6
- queries: bfloat16 [4, 1024, 2048], P(('grp', 'pair'), 'ctx'), parts along dimension 0, may hold values from -64 to 64
- keys: bfloat16 [4, 1024, 1024], P(('grp', 'pair'), 'ctx'), parts along dimension 0, may hold values from -64 to 64
- value_projection: bfloat16 [2688, 1024], P('ctx'), may hold values from -0.125 to 0.125
- adapter_down: bfloat16 [2688, 16], replicated, may hold values from -0.125 to 0.125
- adapter_up: bfloat16 [16, 1024], replicated, may hold values from -1.5 to 1.5
- output_gradient: bfloat16 [4, 1024, 2048], P(('grp', 'pair'), 'ctx'), parts along dimension 0, may hold values from -6 to 6
- policy_logprob: float32 [4, 1024], P(('grp', 'pair'), 'ctx'), parts along dimension 0, may hold values from -6 to 0
- reference_logprob: float32 [4, 1024], P(('grp', 'pair'), 'ctx'), parts along dimension 0, may hold values from -8 to 0
- token_pair_index: int32 [4, 1024], P(('grp', 'pair'), 'ctx'), parts along dimension 0, may hold values from 0 to 7, never falling along the last dimension, each value on 1 to 1017 neighbouring positions
Outputs:
- input_grad: bfloat16 [4, 1024, 2688], P(('grp', 'pair'), 'ctx'), parts along dimension 0
- query_grad: bfloat16 [4, 1024, 2048], P(('grp', 'pair'), 'ctx'), parts along dimension 0
- key_grad: bfloat16 [4, 1024, 1024], P(('grp', 'pair'), 'ctx'), parts along dimension 0
- down_gradient: float32 [5376, 16], P('grp'), parts along dimension 0
- up_gradient: float32 [32, 1024], P('grp'), parts along dimension 0
There are 2 independent parts, one for each index of `grp`. A program takes and returns all parts, laid end to end along the dimension named above; an argument that names none is the same for every part. Nothing has to cross between parts.
Inputs may be any that keep to these rules, and one draw needn't show every extreme that they name: `token_pair_index`: along each sequence the ids never fall; both sequences hold every id, each segment at most 1017 tokens and one exactly 1017.
All inputs are finite; a program needn't handle non-finite values.
Results may differ from a plain program's by a relative error of at most 0.03.
Values may be sent and summed in bfloat16 or wider, within the bound.
No kernel may reach another device: no remote copies, remote signals or barrier semaphores. Data moves between devices by JAX's collectives and lax.ppermute only.
A program may use at most 128 MiB of HBM per device.

v0:
```python
import jax
import jax.numpy as jnp
from jax import lax
from jax.sharding import PartitionSpec as P

HEAD_SIZE = 128
WINDOW = 1024
SEGS = 8
DPO_BETA = 0.1
LOSS_SCALE = 256.0
ADAPTER_SCALE = 2.0
ATTN_SCALE = 168.0 ** (-0.5)
NEG_FILL = -1e30


def from_partner(shard, axis, stride):
    return lax.ppermute(shard, axis, [(i, i ^ 1 << stride) for i in range(lax.axis_size(axis))])


def shifted(block, axis, distance):
    devices = range(lax.axis_size(axis))
    route = [(i - distance, i) for i in devices if i - distance in devices]
    return lax.ppermute(block, axis, route)


def shards(
    normed_input,
    queries,
    keys,
    value_projection,
    adapter_down,
    adapter_up,
    output_gradient,
    policy_logprob,
    reference_logprob,
    token_pair_index,
):
    tok_rows = normed_input.shape[1]
    width_kv = keys.shape[2]
    kv_heads = width_kv // HEAD_SIZE
    group_size = queries.shape[2] // width_kv
    hidden_rows = normed_input[0]
    own_keys = keys[0]
    pair_index = lax.axis_index("pair")
    ctx_index = lax.axis_index("ctx")
    half_cols = width_kv // 2
    own_half = lax.dynamic_slice_in_dim(value_projection, pair_index * half_cols, half_cols, 1)
    rows_half = lax.all_gather(own_half, "ctx", axis=0, tiled=True)
    full_weight = lax.all_gather(rows_half, "pair", axis=1, tiled=True)
    rank_projection = jnp.dot(hidden_rows, adapter_down, preferred_element_type=jnp.float32).astype(
        jnp.bfloat16
    )
    values = (
        jnp.dot(hidden_rows, full_weight, preferred_element_type=jnp.float32)
        + ADAPTER_SCALE * jnp.dot(rank_projection, adapter_up, preferred_element_type=jnp.float32)
    ).astype(jnp.bfloat16)
    segment_labels = token_pair_index[0]
    seg_table = (segment_labels[:, None] == jnp.arange(SEGS, dtype=jnp.int32)[None, :]).astype(
        jnp.float32
    )
    log_gap = policy_logprob[0] - reference_logprob[0]
    part_diff = jnp.sum(seg_table * log_gap[:, None], 0)
    part_count = jnp.sum(seg_table, 0)
    own_diff, counts = lax.psum((part_diff, part_count), "ctx")
    other_diff = from_partner(own_diff, "pair", 0)
    direction = 1.0 - 2.0 * pair_index.astype(jnp.float32)
    margin = DPO_BETA * (direction * (own_diff - other_diff))
    coef = -direction * DPO_BETA * LOSS_SCALE * jax.nn.sigmoid(-margin)
    starts = jnp.cumsum(counts) - counts
    tok_start = jnp.sum(seg_table * starts[None, :], 1).astype(jnp.int32)
    token_coefficient = jnp.sum(seg_table * coef[None, :], 1)
    halo_blocks = min(WINDOW // tok_rows, lax.axis_size("ctx") - 1)
    key_blocks = []
    value_blocks = []
    for distance in range(halo_blocks, 0, -1):
        key_blocks.append(shifted(own_keys, "ctx", distance))
        value_blocks.append(shifted(values, "ctx", distance))
    all_keys = jnp.concatenate(key_blocks + [own_keys], 0)
    all_keys, own_values = lax.optimization_barrier((all_keys, values))
    all_values = jnp.concatenate(value_blocks + [own_values], 0)
    span = all_keys.shape[0]
    tpos = ctx_index * tok_rows + jnp.arange(tok_rows, dtype=jnp.int32)
    upos = ctx_index * tok_rows - halo_blocks * tok_rows + jnp.arange(span, dtype=jnp.int32)
    allowed = (
        (upos[None, :] <= tpos[:, None])
        & (upos[None, :] > tpos[:, None] - WINDOW)
        & (upos[None, :] >= tok_start[:, None])
    )
    coef_rows = token_coefficient[None, :, None]
    query_rows = queries[0].reshape(tok_rows, kv_heads, group_size, HEAD_SIZE)
    grad_rows = output_gradient[0].reshape(tok_rows, kv_heads, group_size, HEAD_SIZE)
    key_rows = all_keys.reshape(span, kv_heads, HEAD_SIZE)
    value_rows = all_values.reshape(span, kv_heads, HEAD_SIZE)
    scores = ATTN_SCALE * jnp.einsum(
        "tjgd,ljd->jgtl", query_rows, key_rows, preferred_element_type=jnp.float32
    )
    masked = jnp.where(allowed[None, None], scores, NEG_FILL)
    row_max = jnp.max(masked, -1, keepdims=True)
    weights_exp = jnp.where(allowed[None, None], jnp.exp(masked - row_max), 0.0)
    attn_probs = weights_exp / jnp.sum(weights_exp, -1, keepdims=True)
    prob_grad = coef_rows[None] * jnp.einsum(
        "tjgd,ljd->jgtl", grad_rows, value_rows, preferred_element_type=jnp.float32
    )
    row_delta = jnp.sum(attn_probs * prob_grad, -1, keepdims=True)
    score_grad = (ATTN_SCALE * attn_probs * (prob_grad - row_delta)).astype(jnp.bfloat16)
    query_grad = (
        jnp.einsum("jgtl,ljd->tjgd", score_grad, key_rows, preferred_element_type=jnp.float32)
        .astype(jnp.bfloat16)
        .reshape(tok_rows, kv_heads * group_size * HEAD_SIZE)
    )
    key_parts = jnp.einsum(
        "jgtl,tjgd->ljd", score_grad, query_rows, preferred_element_type=jnp.float32
    ).reshape(span, width_kv)
    weighted = (attn_probs * coef_rows[None]).astype(jnp.bfloat16)
    value_parts = jnp.einsum(
        "jgtl,tjgd->ljd", weighted, grad_rows, preferred_element_type=jnp.float32
    ).reshape(span, width_kv)
    key_total = key_parts[halo_blocks * tok_rows :]
    value_total = value_parts[halo_blocks * tok_rows :]
    for distance in range(1, halo_blocks + 1):
        block_start = (halo_blocks - distance) * tok_rows
        send_keys = key_parts[block_start : block_start + tok_rows].astype(jnp.bfloat16)
        send_values = value_parts[block_start : block_start + tok_rows].astype(jnp.bfloat16)
        back_keys, back_values = shifted((send_keys, send_values), "ctx", -distance)
        key_total = key_total + back_keys.astype(jnp.float32)
        value_total = value_total + back_values.astype(jnp.float32)
    key_grad = key_total.astype(jnp.bfloat16)
    value_gradient = value_total.astype(jnp.bfloat16)
    rank_middle = jnp.einsum(
        "sj,zj->sz", value_gradient, adapter_up, preferred_element_type=jnp.float32
    ).astype(jnp.bfloat16)
    input_grad = (
        jnp.einsum("tk,dk->td", value_gradient, full_weight, preferred_element_type=jnp.float32)
        + ADAPTER_SCALE
        * jnp.einsum("pb,wb->pw", rank_middle, adapter_down, preferred_element_type=jnp.float32)
    ).astype(jnp.bfloat16)
    up_factor = ADAPTER_SCALE * jnp.einsum(
        "tr,tk->rk", rank_projection, value_gradient, preferred_element_type=jnp.float32
    )
    down_factor = ADAPTER_SCALE * jnp.einsum(
        "td,tr->dr", hidden_rows, rank_middle, preferred_element_type=jnp.float32
    )
    down_gradient, up_gradient = lax.psum((down_factor, up_factor), ("ctx", "pair"))
    return (input_grad[None], query_grad[None], key_grad[None], down_gradient, up_gradient)


def solution(mesh):
    return jax.shard_map(
        shards,
        mesh=mesh,
        in_specs=(
            P(("grp", "pair"), "ctx", None),
            P(("grp", "pair"), "ctx", None),
            P(("grp", "pair"), "ctx", None),
            P("ctx", None),
            P(),
            P(),
            P(("grp", "pair"), "ctx", None),
            P(("grp", "pair"), "ctx"),
            P(("grp", "pair"), "ctx"),
            P(("grp", "pair"), "ctx"),
        ),
        out_specs=(
            P(("grp", "pair"), "ctx", None),
            P(("grp", "pair"), "ctx", None),
            P(("grp", "pair"), "ctx", None),
            P("grp", None),
            P("grp", None),
        ),
        check_vma=False,
    )
```

profile of v0, /device:TPU:8, one launch (start us, length us, event | category | flops | bytes accessed | tf_op | source)
XLA Modules:
  0.0 361.4 jit_solution(16586474015925666652)
XLA Ops:
  9.2 58.9 %all-gather.3.cloned.1.call-done = bf16[2688,512]{1,0:T(8,128)(2,1)} async-done(((bf16[336,512]{1,0:T(8,128)(2,1)}), bf16[2688,512]{1,0:T(8,128)(2,1)}) %all-gather.3.cloned.1.call-update) | async-done | bytes 2752528 | tf_op jit(solution)/shard_map/all_gather | solution.py:48
  70.2 4.2 %collective-permute-start.2 = (bf16[128,1024]{1,0:T(8,128)(2,1)}, bf16[128,1024]{1,0:T(8,128)(2,1)}, u32[]{:S(2)}, u32[]{:S(2)}) collective-permute-start(bf16[128,1024]{1,0:T(8,128)(2,1)} %bitcast.3), channel_id=1, source_target_pairs={{0,10},{2,12},{4,14},{1,11},{3,13},{5,15},{16,26},{18,28},{20,30},... | collective-permute-start | bytes 786440 | tf_op jit(solution)/shard_map/ppermute | solution.py:23
  76.5 30.3 %all-reduce.1 = (f32[8]{0:T(128)S(1)}, f32[8]{0:T(128)S(1)}) all-reduce(f32[8]{0:T(128)S(1)} %get-tuple-element.21, f32[8]{0:T(128)S(1)} %get-tuple-element.22), channel_id=1, replica_groups=mesh['grp'=2,'ctx'=8,'pair'=2] {'ctx'}, use_global_device_ids=true, to_apply=%region_1.0 | all-reduce | flops 16 | bytes 128 | tf_op jit(solution)/shard_map/psum | solution.py:64
  108.8 2.9 collective-permute-start.4
  113.4 3.2 collective-permute-start.5
  122.4 3.8 %collective-permute-done.5 = bf16[128,1024]{1,0:T(8,128)(2,1)S(1)} collective-permute-done((bf16[128,1024]{1,0:T(8,128)(2,1)}, bf16[128,1024]{1,0:T(8,128)(2,1)S(1)}, u32[]{:S(2)}, u32[]{:S(2)}) %collective-permute-start.5) | collective-permute-done | bytes 262176 | tf_op jit(solution)/shard_map/ppermute | solution.py:23
  126.3 4.2 %collective-permute-done.6 = bf16[128,1024]{1,0:T(8,128)(2,1)S(1)} collective-permute-done((bf16[128,1024]{1,0:T(8,128)(2,1)}, bf16[128,1024]{1,0:T(8,128)(2,1)S(1)}, u32[]{:S(2)}, u32[]{:S(2)}) %collective-permute-start.6) | collective-permute-done | bytes 262176 | tf_op jit(solution)/shard_map/ppermute | solution.py:23
  131.5 4.2 %convolution_bitcast_fusion.1 = f32[128,1024]{0,1:T(8,128)S(1)} fusion(bf16[2688,1024]{1,0:T(8,128)(2,1)} %all-gather.5.cloned.1.call-done, bf16[1,128,2688]{2,1,0:T(8,128)(2,1)S(1)} %copy-done), kind=kOutput, calls=%fused_computation.26 | convolution fusion | flops 704643072 | bytes 6717440 | tf_op jit(solution)/shard_map/dot_general | solution.py:54
  139.4 2.3 collective-permute-start.17
  141.6 6.5 %collective-permute-start.18 = (bf16[128,1024]{0,1:T(8,128)(2,1)}, bf16[128,1024]{0,1:T(8,128)(2,1)}, u32[]{:S(2)}, u32[]{:S(2)}) collective-permute-start(bf16[128,1024]{0,1:T(8,128)(2,1)} %fusion.15), channel_id=1, source_target_pairs={{0,8},{2,10},{4,12},{6,14},{1,9},{3,11},{5,13},{7,15},{16,24},{18,... | collective-permute-start | bytes 786440 | tf_op jit(solution)/shard_map/ppermute | solution.py:23
  152.1 3.2 copy.60
  155.4 6.9 %fusion.36 = (f32[8,2,128]{2,1,0:T(2,128)S(1)}, f32[8,2,128,1024]{2,3,1,0:T(8,128)}) fusion(pred[128,1024]{0,1:T(8,128)(4,1)} %compare_and_fusion, bf16[1024,8,128,1]{0,2,3,1:T(8,128)(2,1)S(1)} %copy.60, bf16[128,8,2,128]{0,3,2,1:T(8,128)(2,1)S(1)} %bitcast.126), kind=kOutput, calls=%fused_computation.82 | convolution fusion | flops 547357696 | bytes 11149312 | tf_op jit(solution)/shard_map/sub | solution.py:99
  162.3 5.1 %fusion.37 = (bf16[1024,8,128]{0,2,1:T(8,128)(2,1)S(1)}, f32[1024,8,128]{0,2,1:T(8,128)S(1)}) fusion(bf16[128,8,2,128]{3,2,1,0:T(2,128)(2,1)} %reshape_squeeze.7, f32[128]{0:T(128)S(1)} %get-tuple-element.20, f32[8,2,128,1024]{2,3,1,0:T(8,128)} %get-tuple-element.42, f32[8,2,128]{2,1,0:T(2,128)S(1)} %get-tuple-element.41), kind=kOutput, calls=%fused_computation.83 | convolution fusion | flops 544210944 | bytes 15213056 | tf_op jit(solution)/shard_map/jgtl,tjgd->ljd/dot_general | solution.py:115
  168.0 2.9 collective-permute-start.20
  180.8 3.2 collective-permute-done.20
  193.4 2.9 collective-permute-start.9
  196.3 3.1 collective-permute-start.8
  199.5 3.5 fusion.38
  203.1 19.5 %collective-permute-done.10 = bf16[128,1024]{0,1:T(8,128)(2,1)S(1)} collective-permute-done((bf16[128,1024]{0,1:T(8,128)(2,1)S(1)}, bf16[128,1024]{0,1:T(8,128)(2,1)S(1)}, u32[]{:S(2)}, u32[]{:S(2)}) %collective-permute-start.10) | collective-permute-done | bytes 262176 | tf_op jit(solution)/shard_map/ppermute | solution.py:23
  225.4 2.0 copy.54
  249.4 5.3 %fusion.11 = bf16[1,128,2688]{2,1,0:T(8,128)(2,1)} fusion(f32[128,2688]{1,0:T(8,128)S(1)} %convolution_multiply_fusion, bf16[128,1024]{0,1:T(8,128)(2,1)S(1)} %fusion.27, bf16[2688,1024]{1,0:T(8,128)(2,1)} %all-gather.5.cloned.1.call-done), kind=kOutput, calls=%fused_computation.19 | convolution fusion | flops 705331200 | bytes 7831552 | tf_op jit(solution)/shard_map/tk,dk->td/dot_general | solution.py:133
  254.7 16.3 %collective-permute-done.24 = bf16[128,1024]{1,0:T(8,128)(2,1)} collective-permute-done((bf16[128,1024]{1,0:T(8,128)(2,1)}, bf16[128,1024]{1,0:T(8,128)(2,1)}, u32[]{:S(2)}, u32[]{:S(2)}) %collective-permute-start.24) | collective-permute-done | bytes 262176 | tf_op jit(solution)/shard_map/ppermute | solution.py:23
  271.1 3.9 %collective-permute-done.23 = bf16[128,1024]{1,0:T(8,128)(2,1)S(1)} collective-permute-done((bf16[128,1024]{1,0:T(8,128)(2,1)}, bf16[128,1024]{1,0:T(8,128)(2,1)S(1)}, u32[]{:S(2)}, u32[]{:S(2)}) %collective-permute-start.23) | collective-permute-done | bytes 262176 | tf_op jit(solution)/shard_map/ppermute | solution.py:23
  277.0 74.8 %all-reduce.4.cloned.1.call-done = (f32[2688,16]{0,1:T(8,128)}, f32[16,1024]{1,0:T(8,128)}) async-done(((f32[2688,16]{0,1:T(8,128)}, f32[16,1024]{1,0:T(8,128)}), (f32[2688,16]{0,1:T(8,128)}, f32[16,1024]{1,0:T(8,128)})) %all-reduce.4.cloned.1.call-update) | async-done | bytes 237584 | tf_op jit(solution)/shard_map/psum | solution.py:143
  (137 shorter events, 73.9 us)
Async XLA Ops:
  7.2 60.8 %all-gather.3.cloned.1.call-start = ((), (), s32[]{:S(2)}) async-start(), calls=%async_computation | async-start | bytes 3096576 | tf_op jit(solution)/shard_map/all_gather | solution.py:48
  9.1 122.3 %all-gather.5.cloned.1.call-start = ((), (), s32[]{:S(2)}) async-start(), calls=%async_computation.1 | async-start | bytes 8257536 | tf_op jit(solution)/shard_map/all_gather | solution.py:49
  68.1 283.8 %all-reduce.4.cloned.1.call-start = ((), (), s32[]{:S(2)}) async-start(), calls=%async_computation.2 | async-start | bytes 475136 | tf_op jit(solution)/shard_map/psum | solution.py:143
  68.1 44.5 %collective-permute-start = (bf16[128,1024]{1,0:T(8,128)(2,1)}, bf16[128,1024]{1,0:T(8,128)(2,1)S(1)}, u32[]{:S(2)}, u32[]{:S(2)}) collective-permute-start(bf16[128,1024]{1,0:T(8,128)(2,1)} %bitcast.3), channel_id=1, source_target_pairs={{0,14},{1,15},{16,30},{17,31}} | collective-permute-start | bytes 786440 | tf_op jit(solution)/shard_map/ppermute | solution.py:23
  68.8 48.7 %collective-permute-start.1 = (bf16[128,1024]{1,0:T(8,128)(2,1)}, bf16[128,1024]{1,0:T(8,128)(2,1)}, u32[]{:S(2)}, u32[]{:S(2)}) collective-permute-start(bf16[128,1024]{1,0:T(8,128)(2,1)} %bitcast.3), channel_id=1, source_target_pairs={{0,12},{2,14},{1,13},{3,15},{16,28},{18,30},{17,29},{19,31}} | collective-permute-start | bytes 786440 | tf_op jit(solution)/shard_map/ppermute | solution.py:23
  70.2 50.3 %collective-permute-start.2 = (bf16[128,1024]{1,0:T(8,128)(2,1)}, bf16[128,1024]{1,0:T(8,128)(2,1)}, u32[]{:S(2)}, u32[]{:S(2)}) collective-permute-start(bf16[128,1024]{1,0:T(8,128)(2,1)} %bitcast.3), channel_id=1, source_target_pairs={{0,10},{2,12},{4,14},{1,11},{3,13},{5,15},{16,26},{18,28},{20,30},... | collective-permute-start | bytes 786440 | tf_op jit(solution)/shard_map/ppermute | solution.py:23
  74.3 47.1 %collective-permute-start.3 = (bf16[128,1024]{1,0:T(8,128)(2,1)}, bf16[128,1024]{1,0:T(8,128)(2,1)}, u32[]{:S(2)}, u32[]{:S(2)}) collective-permute-start(bf16[128,1024]{1,0:T(8,128)(2,1)} %bitcast.3), channel_id=1, source_target_pairs={{0,8},{2,10},{4,12},{6,14},{1,9},{3,11},{5,13},{7,15},{16,24},{18,... | collective-permute-start | bytes 786440 | tf_op jit(solution)/shard_map/ppermute | solution.py:23
  136.7 31.4 %collective-permute-start.15 = (bf16[128,1024]{0,1:T(8,128)(2,1)}, bf16[128,1024]{0,1:T(8,128)(2,1)}, u32[]{:S(2)}, u32[]{:S(2)}) collective-permute-start(bf16[128,1024]{0,1:T(8,128)(2,1)} %fusion.15), channel_id=1, source_target_pairs={{0,14},{1,15},{16,30},{17,31}} | collective-permute-start | bytes 786440 | tf_op jit(solution)/shard_map/ppermute | solution.py:23
  138.0 34.0 %collective-permute-start.16 = (bf16[128,1024]{0,1:T(8,128)(2,1)}, bf16[128,1024]{0,1:T(8,128)(2,1)}, u32[]{:S(2)}, u32[]{:S(2)}) collective-permute-start(bf16[128,1024]{0,1:T(8,128)(2,1)} %fusion.15), channel_id=1, source_target_pairs={{0,12},{2,14},{1,13},{3,15},{16,28},{18,30},{17,29},{19,31}} | collective-permute-start | bytes 786440 | tf_op jit(solution)/shard_map/ppermute | solution.py:23
  139.4 35.6 %collective-permute-start.17 = (bf16[128,1024]{0,1:T(8,128)(2,1)}, bf16[128,1024]{0,1:T(8,128)(2,1)}, u32[]{:S(2)}, u32[]{:S(2)}) collective-permute-start(bf16[128,1024]{0,1:T(8,128)(2,1)} %fusion.15), channel_id=1, source_target_pairs={{0,10},{2,12},{4,14},{1,11},{3,13},{5,15},{16,26},{18,28},{20,30},... | collective-permute-start | bytes 786440 | tf_op jit(solution)/shard_map/ppermute | solution.py:23
  141.6 35.1 %collective-permute-start.18 = (bf16[128,1024]{0,1:T(8,128)(2,1)}, bf16[128,1024]{0,1:T(8,128)(2,1)}, u32[]{:S(2)}, u32[]{:S(2)}) collective-permute-start(bf16[128,1024]{0,1:T(8,128)(2,1)} %fusion.15), channel_id=1, source_target_pairs={{0,8},{2,10},{4,12},{6,14},{1,9},{3,11},{5,13},{7,15},{16,24},{18,... | collective-permute-start | bytes 786440 | tf_op jit(solution)/shard_map/ppermute | solution.py:23
  148.2 30.3 %collective-permute-start.19 = (bf16[128,1024]{0,1:T(8,128)(2,1)}, bf16[128,1024]{0,1:T(8,128)(2,1)}, u32[]{:S(2)}, u32[]{:S(2)}) collective-permute-start(bf16[128,1024]{0,1:T(8,128)(2,1)} %fusion.15), channel_id=1, source_target_pairs={{0,6},{2,8},{4,10},{6,12},{8,14},{1,7},{3,9},{5,11},{7,13},{9,15},... | collective-permute-start | bytes 786440 | tf_op jit(solution)/shard_map/ppermute | solution.py:23
  175.0 18.5 %collective-permute-start.14 = (bf16[128,1024]{0,1:T(8,128)(2,1)S(1)}, bf16[128,1024]{0,1:T(8,128)(2,1)S(1)}, u32[]{:S(2)}, u32[]{:S(2)}) collective-permute-start(bf16[128,1024]{0,1:T(8,128)(2,1)S(1)} %bitcast.141), channel_id=1, source_target_pairs={{14,0},{15,1},{30,16},{31,17}} | collective-permute-start | bytes 786440 | tf_op jit(solution)/shard_map/ppermute | solution.py:23
  176.7 19.6 %collective-permute-start.13 = (bf16[128,1024]{0,1:T(8,128)(2,1)S(1)}, bf16[128,1024]{0,1:T(8,128)(2,1)S(1)}, u32[]{:S(2)}, u32[]{:S(2)}) collective-permute-start(bf16[128,1024]{0,1:T(8,128)(2,1)S(1)} %bitcast.140), channel_id=1, source_target_pairs={{12,0},{14,2},{13,1},{15,3},{28,16},{30,18},{29,17},{31,19}} | collective-permute-start | bytes 786440 | tf_op jit(solution)/shard_map/ppermute | solution.py:23
  178.4 24.5 %collective-permute-start.12 = (bf16[128,1024]{0,1:T(8,128)(2,1)S(1)}, bf16[128,1024]{0,1:T(8,128)(2,1)S(1)}, u32[]{:S(2)}, u32[]{:S(2)}) collective-permute-start(bf16[128,1024]{0,1:T(8,128)(2,1)S(1)} %bitcast.139), channel_id=1, source_target_pairs={{10,0},{12,2},{14,4},{11,1},{13,3},{15,5},{26,16},{28,18},{30,20},... | collective-permute-start | bytes 786440 | tf_op jit(solution)/shard_map/ppermute | solution.py:23
  184.0 19.2 %collective-permute-start.11 = (bf16[128,1024]{0,1:T(8,128)(2,1)S(1)}, bf16[128,1024]{0,1:T(8,128)(2,1)S(1)}, u32[]{:S(2)}, u32[]{:S(2)}) collective-permute-start(bf16[128,1024]{0,1:T(8,128)(2,1)S(1)} %bitcast.138), channel_id=1, source_target_pairs={{8,0},{10,2},{12,4},{14,6},{9,1},{11,3},{13,5},{15,7},{24,16},{26,... | collective-permute-start | bytes 786440 | tf_op jit(solution)/shard_map/ppermute | solution.py:23
  185.5 37.2 %collective-permute-start.10 = (bf16[128,1024]{0,1:T(8,128)(2,1)S(1)}, bf16[128,1024]{0,1:T(8,128)(2,1)S(1)}, u32[]{:S(2)}, u32[]{:S(2)}) collective-permute-start(bf16[128,1024]{0,1:T(8,128)(2,1)S(1)} %bitcast.137), channel_id=1, source_target_pairs={{6,0},{8,2},{10,4},{12,6},{14,8},{7,1},{9,3},{11,5},{13,7},{15,9},... | collective-permute-start | bytes 786440 | tf_op jit(solution)/shard_map/ppermute | solution.py:23
  193.4 30.7 %collective-permute-start.9 = (bf16[128,1024]{0,1:T(8,128)(2,1)S(1)}, bf16[128,1024]{0,1:T(8,128)(2,1)S(1)}, u32[]{:S(2)}, u32[]{:S(2)}) collective-permute-start(bf16[128,1024]{0,1:T(8,128)(2,1)S(1)} %bitcast.136), channel_id=1, source_target_pairs={{4,0},{6,2},{8,4},{10,6},{12,8},{14,10},{5,1},{7,3},{9,5},{11,7},{... | collective-permute-start | bytes 786440 | tf_op jit(solution)/shard_map/ppermute | solution.py:23
  196.3 27.8 %collective-permute-start.8 = (bf16[128,1024]{0,1:T(8,128)(2,1)S(1)}, bf16[128,1024]{0,1:T(8,128)(2,1)S(1)}, u32[]{:S(2)}, u32[]{:S(2)}) collective-permute-start(bf16[128,1024]{0,1:T(8,128)(2,1)S(1)} %bitcast.135), channel_id=1, source_target_pairs={{2,0},{4,2},{6,4},{8,6},{10,8},{12,10},{14,12},{3,1},{5,3},{7,5},{... | collective-permute-start | bytes 786440 | tf_op jit(solution)/shard_map/ppermute | solution.py:23
  235.7 19.1 %collective-permute-start.26 = (bf16[128,1024]{1,0:T(8,128)(2,1)}, bf16[128,1024]{1,0:T(8,128)(2,1)S(1)}, u32[]{:S(2)}, u32[]{:S(2)}) collective-permute-start(bf16[128,1024]{1,0:T(8,128)(2,1)} %copy.51), channel_id=1, source_target_pairs={{10,0},{12,2},{14,4},{11,1},{13,3},{15,5},{26,16},{28,18},{30,20},... | collective-permute-start | bytes 786440 | tf_op jit(solution)/shard_map/ppermute | solution.py:23
  238.7 16.0 %collective-permute-start.25 = (bf16[128,1024]{1,0:T(8,128)(2,1)}, bf16[128,1024]{1,0:T(8,128)(2,1)S(1)}, u32[]{:S(2)}, u32[]{:S(2)}) collective-permute-start(bf16[128,1024]{1,0:T(8,128)(2,1)} %copy.50), channel_id=1, source_target_pairs={{8,0},{10,2},{12,4},{14,6},{9,1},{11,3},{13,5},{15,7},{24,16},{26,... | collective-permute-start | bytes 786440 | tf_op jit(solution)/shard_map/ppermute | solution.py:23
  240.8 30.2 %collective-permute-start.24 = (bf16[128,1024]{1,0:T(8,128)(2,1)}, bf16[128,1024]{1,0:T(8,128)(2,1)}, u32[]{:S(2)}, u32[]{:S(2)}) collective-permute-start(bf16[128,1024]{1,0:T(8,128)(2,1)} %copy.49), channel_id=1, source_target_pairs={{6,0},{8,2},{10,4},{12,6},{14,8},{7,1},{9,3},{11,5},{13,7},{15,9},... | collective-permute-start | bytes 786440 | tf_op jit(solution)/shard_map/ppermute | solution.py:23
  245.5 29.5 %collective-permute-start.23 = (bf16[128,1024]{1,0:T(8,128)(2,1)}, bf16[128,1024]{1,0:T(8,128)(2,1)S(1)}, u32[]{:S(2)}, u32[]{:S(2)}) collective-permute-start(bf16[128,1024]{1,0:T(8,128)(2,1)} %copy.48), channel_id=1, source_target_pairs={{4,0},{6,2},{8,4},{10,6},{12,8},{14,10},{5,1},{7,3},{9,5},{11,7},{... | collective-permute-start | bytes 786440 | tf_op jit(solution)/shard_map/ppermute | solution.py:23
  247.4 27.6 %collective-permute-start.22 = (bf16[128,1024]{1,0:T(8,128)(2,1)}, bf16[128,1024]{1,0:T(8,128)(2,1)S(1)}, u32[]{:S(2)}, u32[]{:S(2)}) collective-permute-start(bf16[128,1024]{1,0:T(8,128)(2,1)} %copy.46), channel_id=1, source_target_pairs={{2,0},{4,2},{6,4},{8,6},{10,8},{12,10},{14,12},{3,1},{5,3},{7,5},{... | collective-permute-start | bytes 786440 | tf_op jit(solution)/shard_map/ppermute | solution.py:23
  (23 other events, 757.6 us)
Sparse Core Ops, SparseCore 0:
  10.8 57.1 all-gather.2
  69.6 14.4 all-gather.4
  245.2 106.5 all-reduce.3
where the time goes:
time: 363 us; the launch traced here: 361 us
  waiting for transfers between devices  187 us (52%)
  starting transfers between devices  55.1 us (15%)
  local copies, waits for them, and re-layouts  37.7 us (10%)
  matrix products  32 us (9%)
  blocking collectives  30.3 us (8%)
  between operations  14.4 us (4%)
  other arithmetic  5.29 us (1%)
    psum x1, waiting for transfers between devices, shards(): lax.psum((down_factor, up_factor), ('ctx', 'pair'))  74.8 us
    all_gather x1, waiting for transfers between devices, shards(): rows_half = lax.all_gather(own_half, 'ctx', axis=0, tiled=True)  58.9 us
    ppermute x28, starting transfers between devices, shifted(): return lax.ppermute(block, axis, route)  55 us
    ppermute x28, waiting for transfers between devices, shifted(): return lax.ppermute(block, axis, route)  52.8 us
    psum x1, blocking collectives, shards(): own_diff, counts = lax.psum((part_diff, part_count), 'ctx')  30.3 us
    unnamed x48, local copies, waits for them, and re-layouts  17.1 us
    convert_element_type x7, local copies, waits for them, and re-layouts, shards(): key_parts[block_start:block_start + tok_rows].astype(jnp.bfloat16)  8.84 us
  transfers between devices with their start and end apart: 32, of which 11 were waited for; matrix products, arithmetic and copies ran while one was open for 16% of the time, Pallas kernels for 0%

commit v1 on v0

--- a/solution.py
+++ b/solution.py
@@ -11,6 +11,28 @@
 ADAPTER_SCALE = 2.0
 ATTN_SCALE = 168.0 ** (-0.5)
 NEG_FILL = -1e30
+
+
+def in_order(blocks, dim):
+    dims = list(blocks.shape[1:])
+    dims[dim] *= blocks.shape[0]
+    return jnp.moveaxis(blocks, 0, dim).reshape(dims)
+
+
+def ring_gather(x, axis, dim):
+    size = lax.axis_size(axis)
+    pairs = [(i, (i + 1) % size) for i in range(size)]
+    back = [(b, a) for a, b in pairs]
+    lower, upper = ([], [])
+    for lap in range(size - 1):
+        if lap % 2 == 0:
+            lower.append(lax.ppermute(lower[-1] if lower else x, axis, pairs))
+        else:
+            upper.append(lax.ppermute(upper[-1] if upper else x, axis, back))
+    pieces = jnp.stack([*lower[::-1], x, *upper])
+    shift = lax.axis_index(axis) - len(lower)
+    pieces = pieces[(jnp.arange(size) - shift) % size]
+    return in_order(pieces, dim)
 
 
 def from_partner(shard, axis, stride):
@@ -45,7 +67,7 @@
     ctx_index = lax.axis_index("ctx")
     half_cols = width_kv // 2
     own_half = lax.dynamic_slice_in_dim(value_projection, pair_index * half_cols, half_cols, 1)
-    rows_half = lax.all_gather(own_half, "ctx", axis=0, tiled=True)
+    rows_half = ring_gather(own_half, "ctx", 0)
     full_weight = lax.all_gather(rows_half, "pair", axis=1, tiled=True)
     rank_projection = jnp.dot(hidden_rows, adapter_down, preferred_element_type=jnp.float32).astype(
         jnp.bfloat16

time: 363 us -> 370 us (1.019)
  waiting for transfers between devices: 187 us -> 170 us
  starting transfers between devices: 55.1 us -> 71.9 us
  local copies, waits for them, and re-layouts: 37.7 us -> 46.1 us
    all_gather x1 -> x0, waiting for transfers between devices: 58.9 us -> none  [shards(): rows_half = lax.all_gather(own_half, 'ctx', axis=0, tiled=True)]
    ppermute x0 -> x7, waiting for transfers between devices: none -> 43.4 us  [the longest x4 33.7 us: ring_gather(): lower.append(lax.ppermute(lower[-1] if lower else x, axis, pairs))]
    ppermute x0 -> x7, starting transfers between devices: none -> 10.9 us  [the longest x3 6.27 us: ring_gather(): upper.append(lax.ppermute(upper[-1] if upper else x, axis, back))]
    ppermute x28, starting transfers between devices: 55 us -> 60.9 us  [shifted(): return lax.ppermute(block, axis, route)]
    unnamed x48 -> x65, local copies, waits for them, and re-layouts: 17.1 us -> 23 us
  transfers between devices with their start and end apart: 32 -> 38, of which waited for: 11 -> 17; matrix products, arithmetic and copies ran while one was open for 16% -> 17% of each run, Pallas kernels for 0% -> 0%
where the time goes in v1:
time: 370 us; the launch traced here: 369 us
  waiting for transfers between devices  170 us (46%)
  starting transfers between devices  71.9 us (19%)
  local copies, waits for them, and re-layouts  46.1 us (12%)
  matrix products  32 us (9%)
  blocking collectives  28.7 us (8%)
  between operations  14.7 us (4%)
  other arithmetic  5.32 us (1%)
    psum x1, waiting for transfers between devices, shards(): lax.psum((down_factor, up_factor), ('ctx', 'pair'))  73.5 us
    ppermute x28, starting transfers between devices, shifted(): return lax.ppermute(block, axis, route)  60.9 us
    ppermute x28, waiting for transfers between devices, shifted(): return lax.ppermute(block, axis, route)  52.9 us
    ppermute x4, waiting for transfers between devices, ring_gather(): lower.append(lax.ppermute(lower[-1] if lower else x, axis, pairs))  33.7 us
    psum x1, blocking collectives, shards(): own_diff, counts = lax.psum((part_diff, part_count), 'ctx')  28.7 us
    unnamed x65, local copies, waits for them, and re-layouts  23 us
    convert_element_type x7, local copies, waits for them, and re-layouts, shards(): key_parts[block_start:block_start + tok_rows].astype(jnp.bfloat16)  9.84 us
    ppermute x3, waiting for transfers between devices, ring_gather(): upper.append(lax.ppermute(upper[-1] if upper else x, axis, back))  9.64 us
  transfers between devices with their start and end apart: 38, of which 17 were waited for; matrix products, arithmetic and copies ran while one was open for 17% of the time, Pallas kernels for 0%

profile of v1, /device:TPU:8, one launch (start us, length us, event | category | flops | bytes accessed | tf_op | source)
XLA Modules:
  0.0 368.7 jit_solution(17221334742173083109)
XLA Ops:
  9.8 9.2 %collective-permute-done.7 = bf16[336,512]{1,0:T(8,128)(2,1)S(1)} collective-permute-done((bf16[336,512]{1,0:T(8,128)(2,1)S(1)}, bf16[336,512]{1,0:T(8,128)(2,1)S(1)}, u32[]{:S(2)}, u32[]{:S(2)}) %collective-permute-start.7) | collective-permute-done | bytes 344096 | tf_op jit(solution)/shard_map/ppermute | solution.py:29
  22.7 11.5 %collective-permute-done.8 = bf16[336,512]{1,0:T(8,128)(2,1)S(1)} collective-permute-done((bf16[336,512]{1,0:T(8,128)(2,1)S(1)}, bf16[336,512]{1,0:T(8,128)(2,1)S(1)}, u32[]{:S(2)}, u32[]{:S(2)}) %collective-permute-start.8) | collective-permute-done | bytes 344096 | tf_op jit(solution)/shard_map/ppermute | solution.py:29
  39.2 6.4 %collective-permute-done.9 = bf16[336,512]{1,0:T(8,128)(2,1)S(1)} collective-permute-done((bf16[336,512]{1,0:T(8,128)(2,1)S(1)}, bf16[336,512]{1,0:T(8,128)(2,1)S(1)}, u32[]{:S(2)}, u32[]{:S(2)}) %collective-permute-start.9) | collective-permute-done | bytes 344096 | tf_op jit(solution)/shard_map/ppermute | solution.py:29
  45.6 7.3 %collective-permute-done.12 = bf16[336,512]{1,0:T(8,128)(2,1)} collective-permute-done((bf16[336,512]{1,0:T(8,128)(2,1)S(1)}, bf16[336,512]{1,0:T(8,128)(2,1)}, u32[]{:S(2)}, u32[]{:S(2)}) %collective-permute-start.12) | collective-permute-done | bytes 344096 | tf_op jit(solution)/shard_map/ppermute | solution.py:31
  54.7 6.7 %collective-permute-done.10 = bf16[336,512]{1,0:T(8,128)(2,1)} collective-permute-done((bf16[336,512]{1,0:T(8,128)(2,1)S(1)}, bf16[336,512]{1,0:T(8,128)(2,1)}, u32[]{:S(2)}, u32[]{:S(2)}) %collective-permute-start.10) | collective-permute-done | bytes 344096 | tf_op jit(solution)/shard_map/ppermute | solution.py:29
  73.1 10.0 %collective-permute-start.2 = (bf16[128,1024]{1,0:T(8,128)(2,1)}, bf16[128,1024]{1,0:T(8,128)(2,1)}, u32[]{:S(2)}, u32[]{:S(2)}) collective-permute-start(bf16[128,1024]{1,0:T(8,128)(2,1)} %bitcast.3), channel_id=1, source_target_pairs={{0,10},{2,12},{4,14},{1,11},{3,13},{5,15},{16,26},{18,28},{20,30},... | collective-permute-start | bytes 786440 | tf_op jit(solution)/shard_map/ppermute | solution.py:45
  85.2 28.7 %all-reduce.1 = (f32[8]{0:T(128)S(1)}, f32[8]{0:T(128)S(1)}) all-reduce(f32[8]{0:T(128)S(1)} %get-tuple-element.21, f32[8]{0:T(128)S(1)} %get-tuple-element.22), channel_id=1, replica_groups=mesh['grp'=2,'ctx'=8,'pair'=2] {'ctx'}, use_global_device_ids=true, to_apply=%region_1.2 | all-reduce | flops 16 | bytes 128 | tf_op jit(solution)/shard_map/psum | solution.py:86
  120.5 3.2 collective-permute-start.5
  129.6 3.8 %collective-permute-done.5 = bf16[128,1024]{1,0:T(8,128)(2,1)S(1)} collective-permute-done((bf16[128,1024]{1,0:T(8,128)(2,1)}, bf16[128,1024]{1,0:T(8,128)(2,1)S(1)}, u32[]{:S(2)}, u32[]{:S(2)}) %collective-permute-start.5) | collective-permute-done | bytes 262176 | tf_op jit(solution)/shard_map/ppermute | solution.py:45
  133.4 4.2 %collective-permute-done.6 = bf16[128,1024]{1,0:T(8,128)(2,1)S(1)} collective-permute-done((bf16[128,1024]{1,0:T(8,128)(2,1)}, bf16[128,1024]{1,0:T(8,128)(2,1)S(1)}, u32[]{:S(2)}, u32[]{:S(2)}) %collective-permute-start.6) | collective-permute-done | bytes 262176 | tf_op jit(solution)/shard_map/ppermute | solution.py:45
  138.6 4.2 %convolution_bitcast_fusion.1 = f32[128,1024]{0,1:T(8,128)S(1)} fusion(bf16[2688,1024]{1,0:T(8,128)(2,1)} %all-gather.2.cloned.1.call-done, bf16[1,128,2688]{2,1,0:T(8,128)(2,1)S(1)} %copy-done), kind=kOutput, calls=%fused_computation.27 | convolution fusion | flops 704643072 | bytes 6717440 | tf_op jit(solution)/shard_map/dot_general | solution.py:76
  148.8 6.5 %collective-permute-start.25 = (bf16[128,1024]{0,1:T(8,128)(2,1)}, bf16[128,1024]{0,1:T(8,128)(2,1)}, u32[]{:S(2)}, u32[]{:S(2)}) collective-permute-start(bf16[128,1024]{0,1:T(8,128)(2,1)} %fusion.15), channel_id=1, source_target_pairs={{0,8},{2,10},{4,12},{6,14},{1,9},{3,11},{5,13},{7,15},{16,24},{18,... | collective-permute-start | bytes 786440 | tf_op jit(solution)/shard_map/ppermute | solution.py:45
  159.3 3.2 copy.60
  162.5 6.9 %fusion.38 = (f32[8,2,128]{2,1,0:T(2,128)S(1)}, f32[8,2,128,1024]{2,3,1,0:T(8,128)}) fusion(pred[128,1024]{0,1:T(8,128)(4,1)} %compare_and_fusion, bf16[1024,8,128,1]{0,2,3,1:T(8,128)(2,1)S(1)} %copy.60, bf16[128,8,2,128]{0,3,2,1:T(8,128)(2,1)S(1)} %bitcast.146), kind=kOutput, calls=%fused_computation.98 | convolution fusion | flops 547357696 | bytes 11149312 | tf_op jit(solution)/shard_map/sub | solution.py:121
  169.4 5.1 %fusion.39 = (bf16[1024,8,128]{0,2,1:T(8,128)(2,1)S(1)}, f32[1024,8,128]{0,2,1:T(8,128)S(1)}) fusion(bf16[128,8,2,128]{3,2,1,0:T(2,128)(2,1)} %reshape_squeeze.7, f32[128]{0:T(128)S(1)} %get-tuple-element.20, f32[8,2,128,1024]{2,3,1,0:T(8,128)} %get-tuple-element.42, f32[8,2,128]{2,1,0:T(2,128)S(1)} %get-tuple-element.41), kind=kOutput, calls=%fused_computation.99 | convolution fusion | flops 544210944 | bytes 15213056 | tf_op jit(solution)/shard_map/jgtl,tjgd->ljd/dot_general | solution.py:137
  175.2 2.9 collective-permute-start.27
  187.9 3.2 collective-permute-done.27
  203.5 3.1 collective-permute-start.15
  206.6 3.4 fusion.40
  210.3 19.5 %collective-permute-done.17 = bf16[128,1024]{0,1:T(8,128)(2,1)S(1)} collective-permute-done((bf16[128,1024]{0,1:T(8,128)(2,1)S(1)}, bf16[128,1024]{0,1:T(8,128)(2,1)S(1)}, u32[]{:S(2)}, u32[]{:S(2)}) %collective-permute-start.17) | collective-permute-done | bytes 262176 | tf_op jit(solution)/shard_map/ppermute | solution.py:45
  257.5 5.3 %fusion.11 = bf16[1,128,2688]{2,1,0:T(8,128)(2,1)} fusion(f32[128,2688]{1,0:T(8,128)S(1)} %convolution_multiply_fusion, bf16[128,1024]{0,1:T(8,128)(2,1)S(1)} %fusion.27, bf16[2688,1024]{1,0:T(8,128)(2,1)} %all-gather.2.cloned.1.call-done), kind=kOutput, calls=%fused_computation.20 | convolution fusion | flops 705331200 | bytes 7831552 | tf_op jit(solution)/shard_map/tk,dk->td/dot_general | solution.py:155
  262.9 15.2 %collective-permute-done.31 = bf16[128,1024]{1,0:T(8,128)(2,1)} collective-permute-done((bf16[128,1024]{1,0:T(8,128)(2,1)}, bf16[128,1024]{1,0:T(8,128)(2,1)}, u32[]{:S(2)}, u32[]{:S(2)}) %collective-permute-start.31) | collective-permute-done | bytes 262176 | tf_op jit(solution)/shard_map/ppermute | solution.py:45
  278.1 5.2 %collective-permute-done.30 = bf16[128,1024]{1,0:T(8,128)(2,1)S(1)} collective-permute-done((bf16[128,1024]{1,0:T(8,128)(2,1)}, bf16[128,1024]{1,0:T(8,128)(2,1)S(1)}, u32[]{:S(2)}, u32[]{:S(2)}) %collective-permute-start.30) | collective-permute-done | bytes 262176 | tf_op jit(solution)/shard_map/ppermute | solution.py:45
  285.3 73.5 %all-reduce.4.cloned.1.call-done = (f32[2688,16]{0,1:T(8,128)}, f32[16,1024]{1,0:T(8,128)}) async-done(((f32[2688,16]{0,1:T(8,128)}, f32[16,1024]{1,0:T(8,128)}), (f32[2688,16]{0,1:T(8,128)}, f32[16,1024]{1,0:T(8,128)})) %all-reduce.4.cloned.1.call-update) | async-done | bytes 237584 | tf_op jit(solution)/shard_map/psum | solution.py:165
  (169 shorter events, 105.6 us)
Async XLA Ops:
  7.2 131.4 %all-gather.2.cloned.1.call-start = ((), (), s32[]{:S(2)}) async-start(), calls=%async_computation | async-start | bytes 8257536 | tf_op jit(solution)/shard_map/all_gather | solution.py:71
  20.4 16.6 %collective-permute-start.11 = (bf16[336,512]{1,0:T(8,128)(2,1)S(1)}, bf16[336,512]{1,0:T(8,128)(2,1)S(1)}, u32[]{:S(2)}, u32[]{:S(2)}) collective-permute-start(bf16[336,512]{1,0:T(8,128)(2,1)S(1)} %constant_dynamic-slice_fusion), channel_id=1, source_target_pairs={{2,0},{4,2},{6,4},{8,6},{10,8},{12,10},{14,12},{0,14},{3,1},{5,3},... | collective-permute-start | bytes 1032200 | tf_op jit(solution)/shard_map/ppermute | solution.py:31
  70.8 287.9 %all-reduce.4.cloned.1.call-start = ((), (), s32[]{:S(2)}) async-start(), calls=%async_computation.1 | async-start | bytes 475136 | tf_op jit(solution)/shard_map/psum | solution.py:165
  70.9 48.9 %collective-permute-start = (bf16[128,1024]{1,0:T(8,128)(2,1)}, bf16[128,1024]{1,0:T(8,128)(2,1)S(1)}, u32[]{:S(2)}, u32[]{:S(2)}) collective-permute-start(bf16[128,1024]{1,0:T(8,128)(2,1)} %bitcast.3), channel_id=1, source_target_pairs={{0,14},{1,15},{16,30},{17,31}} | collective-permute-start | bytes 786440 | tf_op jit(solution)/shard_map/ppermute | solution.py:45
  71.7 52.9 %collective-permute-start.1 = (bf16[128,1024]{1,0:T(8,128)(2,1)}, bf16[128,1024]{1,0:T(8,128)(2,1)}, u32[]{:S(2)}, u32[]{:S(2)}) collective-permute-start(bf16[128,1024]{1,0:T(8,128)(2,1)} %bitcast.3), channel_id=1, source_target_pairs={{0,12},{2,14},{1,13},{3,15},{16,28},{18,30},{17,29},{19,31}} | collective-permute-start | bytes 786440 | tf_op jit(solution)/shard_map/ppermute | solution.py:45
  73.1 54.5 %collective-permute-start.2 = (bf16[128,1024]{1,0:T(8,128)(2,1)}, bf16[128,1024]{1,0:T(8,128)(2,1)}, u32[]{:S(2)}, u32[]{:S(2)}) collective-permute-start(bf16[128,1024]{1,0:T(8,128)(2,1)} %bitcast.3), channel_id=1, source_target_pairs={{0,10},{2,12},{4,14},{1,11},{3,13},{5,15},{16,26},{18,28},{20,30},... | collective-permute-start | bytes 786440 | tf_op jit(solution)/shard_map/ppermute | solution.py:45
  83.1 45.5 %collective-permute-start.3 = (bf16[128,1024]{1,0:T(8,128)(2,1)}, bf16[128,1024]{1,0:T(8,128)(2,1)}, u32[]{:S(2)}, u32[]{:S(2)}) collective-permute-start(bf16[128,1024]{1,0:T(8,128)(2,1)} %bitcast.3), channel_id=1, source_target_pairs={{0,8},{2,10},{4,12},{6,14},{1,9},{3,11},{5,13},{7,15},{16,24},{18,... | collective-permute-start | bytes 786440 | tf_op jit(solution)/shard_map/ppermute | solution.py:45
  143.8 31.4 %collective-permute-start.22 = (bf16[128,1024]{0,1:T(8,128)(2,1)}, bf16[128,1024]{0,1:T(8,128)(2,1)}, u32[]{:S(2)}, u32[]{:S(2)}) collective-permute-start(bf16[128,1024]{0,1:T(8,128)(2,1)} %fusion.15), channel_id=1, source_target_pairs={{0,14},{1,15},{16,30},{17,31}} | collective-permute-start | bytes 786440 | tf_op jit(solution)/shard_map/ppermute | solution.py:45
  145.2 34.0 %collective-permute-start.23 = (bf16[128,1024]{0,1:T(8,128)(2,1)}, bf16[128,1024]{0,1:T(8,128)(2,1)}, u32[]{:S(2)}, u32[]{:S(2)}) collective-permute-start(bf16[128,1024]{0,1:T(8,128)(2,1)} %fusion.15), channel_id=1, source_target_pairs={{0,12},{2,14},{1,13},{3,15},{16,28},{18,30},{17,29},{19,31}} | collective-permute-start | bytes 786440 | tf_op jit(solution)/shard_map/ppermute | solution.py:45
  146.5 35.6 %collective-permute-start.24 = (bf16[128,1024]{0,1:T(8,128)(2,1)}, bf16[128,1024]{0,1:T(8,128)(2,1)}, u32[]{:S(2)}, u32[]{:S(2)}) collective-permute-start(bf16[128,1024]{0,1:T(8,128)(2,1)} %fusion.15), channel_id=1, source_target_pairs={{0,10},{2,12},{4,14},{1,11},{3,13},{5,15},{16,26},{18,28},{20,30},... | collective-permute-start | bytes 786440 | tf_op jit(solution)/shard_map/ppermute | solution.py:45
  148.8 35.1 %collective-permute-start.25 = (bf16[128,1024]{0,1:T(8,128)(2,1)}, bf16[128,1024]{0,1:T(8,128)(2,1)}, u32[]{:S(2)}, u32[]{:S(2)}) collective-permute-start(bf16[128,1024]{0,1:T(8,128)(2,1)} %fusion.15), channel_id=1, source_target_pairs={{0,8},{2,10},{4,12},{6,14},{1,9},{3,11},{5,13},{7,15},{16,24},{18,... | collective-permute-start | bytes 786440 | tf_op jit(solution)/shard_map/ppermute | solution.py:45
  155.3 30.3 %collective-permute-start.26 = (bf16[128,1024]{0,1:T(8,128)(2,1)}, bf16[128,1024]{0,1:T(8,128)(2,1)}, u32[]{:S(2)}, u32[]{:S(2)}) collective-permute-start(bf16[128,1024]{0,1:T(8,128)(2,1)} %fusion.15), channel_id=1, source_target_pairs={{0,6},{2,8},{4,10},{6,12},{8,14},{1,7},{3,9},{5,11},{7,13},{9,15},... | collective-permute-start | bytes 786440 | tf_op jit(solution)/shard_map/ppermute | solution.py:45
  182.1 18.5 %collective-permute-start.21 = (bf16[128,1024]{0,1:T(8,128)(2,1)S(1)}, bf16[128,1024]{0,1:T(8,128)(2,1)S(1)}, u32[]{:S(2)}, u32[]{:S(2)}) collective-permute-start(bf16[128,1024]{0,1:T(8,128)(2,1)S(1)} %bitcast.161), channel_id=1, source_target_pairs={{14,0},{15,1},{30,16},{31,17}} | collective-permute-start | bytes 786440 | tf_op jit(solution)/shard_map/ppermute | solution.py:45
  183.9 19.6 %collective-permute-start.20 = (bf16[128,1024]{0,1:T(8,128)(2,1)S(1)}, bf16[128,1024]{0,1:T(8,128)(2,1)S(1)}, u32[]{:S(2)}, u32[]{:S(2)}) collective-permute-start(bf16[128,1024]{0,1:T(8,128)(2,1)S(1)} %bitcast.160), channel_id=1, source_target_pairs={{12,0},{14,2},{13,1},{15,3},{28,16},{30,18},{29,17},{31,19}} | collective-permute-start | bytes 786440 | tf_op jit(solution)/shard_map/ppermute | solution.py:45
  185.6 24.5 %collective-permute-start.19 = (bf16[128,1024]{0,1:T(8,128)(2,1)S(1)}, bf16[128,1024]{0,1:T(8,128)(2,1)S(1)}, u32[]{:S(2)}, u32[]{:S(2)}) collective-permute-start(bf16[128,1024]{0,1:T(8,128)(2,1)S(1)} %bitcast.159), channel_id=1, source_target_pairs={{10,0},{12,2},{14,4},{11,1},{13,3},{15,5},{26,16},{28,18},{30,20},... | collective-permute-start | bytes 786440 | tf_op jit(solution)/shard_map/ppermute | solution.py:45
  191.1 19.2 %collective-permute-start.18 = (bf16[128,1024]{0,1:T(8,128)(2,1)S(1)}, bf16[128,1024]{0,1:T(8,128)(2,1)S(1)}, u32[]{:S(2)}, u32[]{:S(2)}) collective-permute-start(bf16[128,1024]{0,1:T(8,128)(2,1)S(1)} %bitcast.158), channel_id=1, source_target_pairs={{8,0},{10,2},{12,4},{14,6},{9,1},{11,3},{13,5},{15,7},{24,16},{26,... | collective-permute-start | bytes 786440 | tf_op jit(solution)/shard_map/ppermute | solution.py:45
  192.6 37.2 %collective-permute-start.17 = (bf16[128,1024]{0,1:T(8,128)(2,1)S(1)}, bf16[128,1024]{0,1:T(8,128)(2,1)S(1)}, u32[]{:S(2)}, u32[]{:S(2)}) collective-permute-start(bf16[128,1024]{0,1:T(8,128)(2,1)S(1)} %bitcast.157), channel_id=1, source_target_pairs={{6,0},{8,2},{10,4},{12,6},{14,8},{7,1},{9,3},{11,5},{13,7},{15,9},... | collective-permute-start | bytes 786440 | tf_op jit(solution)/shard_map/ppermute | solution.py:45
  200.6 30.7 %collective-permute-start.16 = (bf16[128,1024]{0,1:T(8,128)(2,1)S(1)}, bf16[128,1024]{0,1:T(8,128)(2,1)S(1)}, u32[]{:S(2)}, u32[]{:S(2)}) collective-permute-start(bf16[128,1024]{0,1:T(8,128)(2,1)S(1)} %bitcast.156), channel_id=1, source_target_pairs={{4,0},{6,2},{8,4},{10,6},{12,8},{14,10},{5,1},{7,3},{9,5},{11,7},{... | collective-permute-start | bytes 786440 | tf_op jit(solution)/shard_map/ppermute | solution.py:45
  203.5 27.8 %collective-permute-start.15 = (bf16[128,1024]{0,1:T(8,128)(2,1)S(1)}, bf16[128,1024]{0,1:T(8,128)(2,1)S(1)}, u32[]{:S(2)}, u32[]{:S(2)}) collective-permute-start(bf16[128,1024]{0,1:T(8,128)(2,1)S(1)} %bitcast.155), channel_id=1, source_target_pairs={{2,0},{4,2},{6,4},{8,6},{10,8},{12,10},{14,12},{3,1},{5,3},{7,5},{... | collective-permute-start | bytes 786440 | tf_op jit(solution)/shard_map/ppermute | solution.py:45
  242.8 20.1 %collective-permute-start.33 = (bf16[128,1024]{1,0:T(8,128)(2,1)}, bf16[128,1024]{1,0:T(8,128)(2,1)S(1)}, u32[]{:S(2)}, u32[]{:S(2)}) collective-permute-start(bf16[128,1024]{1,0:T(8,128)(2,1)} %copy.51), channel_id=1, source_target_pairs={{10,0},{12,2},{14,4},{11,1},{13,3},{15,5},{26,16},{28,18},{30,20},... | collective-permute-start | bytes 786440 | tf_op jit(solution)/shard_map/ppermute | solution.py:45
  246.8 16.1 %collective-permute-start.32 = (bf16[128,1024]{1,0:T(8,128)(2,1)}, bf16[128,1024]{1,0:T(8,128)(2,1)S(1)}, u32[]{:S(2)}, u32[]{:S(2)}) collective-permute-start(bf16[128,1024]{1,0:T(8,128)(2,1)} %copy.50), channel_id=1, source_target_pairs={{8,0},{10,2},{12,4},{14,6},{9,1},{11,3},{13,5},{15,7},{24,16},{26,... | collective-permute-start | bytes 786440 | tf_op jit(solution)/shard_map/ppermute | solution.py:45
  249.0 29.1 %collective-permute-start.31 = (bf16[128,1024]{1,0:T(8,128)(2,1)}, bf16[128,1024]{1,0:T(8,128)(2,1)}, u32[]{:S(2)}, u32[]{:S(2)}) collective-permute-start(bf16[128,1024]{1,0:T(8,128)(2,1)} %copy.49), channel_id=1, source_target_pairs={{6,0},{8,2},{10,4},{12,6},{14,8},{7,1},{9,3},{11,5},{13,7},{15,9},... | collective-permute-start | bytes 786440 | tf_op jit(solution)/shard_map/ppermute | solution.py:45
  253.7 29.6 %collective-permute-start.30 = (bf16[128,1024]{1,0:T(8,128)(2,1)}, bf16[128,1024]{1,0:T(8,128)(2,1)S(1)}, u32[]{:S(2)}, u32[]{:S(2)}) collective-permute-start(bf16[128,1024]{1,0:T(8,128)(2,1)} %copy.48), channel_id=1, source_target_pairs={{4,0},{6,2},{8,4},{10,6},{12,8},{14,10},{5,1},{7,3},{9,5},{11,7},{... | collective-permute-start | bytes 786440 | tf_op jit(solution)/shard_map/ppermute | solution.py:45
  255.6 27.7 %collective-permute-start.29 = (bf16[128,1024]{1,0:T(8,128)(2,1)}, bf16[128,1024]{1,0:T(8,128)(2,1)S(1)}, u32[]{:S(2)}, u32[]{:S(2)}) collective-permute-start(bf16[128,1024]{1,0:T(8,128)(2,1)} %copy.46), channel_id=1, source_target_pairs={{2,0},{4,2},{6,4},{8,6},{10,8},{12,10},{14,12},{3,1},{5,3},{7,5},{... | collective-permute-start | bytes 786440 | tf_op jit(solution)/shard_map/ppermute | solution.py:45
  (34 other events, 626.7 us)
Sparse Core Ops, SparseCore 0:
  71.0 20.3 all-gather.1
  253.4 105.3 all-reduce.3
